TPU v7x, 32 devices: a whole 2x2x4 slice. The times are simulated.
32 devices in a mesh: band: 16 (over z, x, core), chan: 2 (over y).
Axes of the slice: x: 2, y: 2, z: 4, core: 2. Of those that a mesh axis runs over, the one named last changes fastest.
Arguments:
- features: bfloat16 [256, 64, 1024], P('chan', 'band'), may hold values from -6 to 6
- depth_kernel: bfloat16 [3, 9, 256], P(None, None, 'chan'), may hold values from -2 to 2
- pointwise: bfloat16 [4, 256, 256], P(None, 'chan'), may hold values from -0.25 to 0.25
- cotangent: bfloat16 [256, 64, 1024], P('chan', 'band'), may hold values from -6 to 6
Outputs:
- output: bfloat16 [256, 64, 1024], P('chan', 'band')
- grad_input: float32 [256, 64, 1024], P('chan', 'band')
- grad_depth: float32 [3, 9, 256], P(None, None, 'chan')
- grad_point: float32 [4, 256, 256], P(None, 'chan')
All inputs are finite; a program needn't handle non-finite values.
Results may differ from a plain program's by a relative error of at most 0.0057.
Values may be sent and summed in bfloat16 or wider, within the bound.
No kernel may reach another device: no remote copies, remote signals or barrier semaphores. Data moves between devices by JAX's collectives and lax.ppermute only.
A program may use at most 128 MiB of HBM per device.

v0:
```python
import jax
import jax.numpy as jnp
from jax import lax
from jax.sharding import PartitionSpec as P


GSCALE = 1024


dilations = (6, 12, 18)


def shifted(block, axis, distance):
    devices = range(lax.axis_size(axis))
    route = [(i - distance, i) for i in devices if i - distance in devices]
    if not route:
        return jnp.zeros_like(block)
    return lax.ppermute(block, axis, route)


def pieces_of(height, offset):
    ahead, start = divmod(offset, height)
    if start == 0:
        return [(ahead, 0, height)]
    return [(ahead, start, height), (ahead + 1, 0, start)]


def halo_rows(requests):
    groups = {}
    for key, (field, offset) in requests.items():
        for ahead, first, last in pieces_of(field.shape[1], offset):
            groups.setdefault((ahead, last - first), []).append((key, field, first, last))
    got = {}
    for (ahead, rows), members in groups.items():
        blocks = [field[:, first:last] for _, field, first, last in members]
        joined = jnp.concatenate(blocks, axis=0) if len(blocks) > 1 else blocks[0]
        if ahead != 0:
            joined = shifted(joined, "band", -ahead)
        at = 0
        for (key, field, first, last), block in zip(members, blocks):
            got.setdefault(key, []).append((first, joined[at : at + block.shape[0]]))
            at += block.shape[0]
    out = {}
    for key, (field, offset) in requests.items():
        parts = got[key]
        out[key] = parts[0][1] if len(parts) == 1 else jnp.concatenate([p for _, p in parts], axis=1)
    return out


def chan_shift(block, s):
    count = lax.axis_size("chan")
    return lax.ppermute(block, "chan", [(j, (j + s) % count) for j in range(count)])


def block(features, depth_kernel, pointwise, cotangent):
    kernel = depth_kernel.astype(jnp.float32)
    count = lax.axis_size("chan")
    width = pointwise.shape[2] // count
    cot_full = jnp.concatenate(
        [cotangent] + [chan_shift(cotangent, s) for s in range(1, count)], axis=0
    )
    requests = {}
    for spacing in dilations:
        for side in (-1, 1):
            requests[side * spacing] = (features, side * spacing)
    feat_halo = halo_rows(requests)
    me = lax.axis_index("chan")
    pw_slots = [
        lax.dynamic_slice_in_dim(pointwise, ((me - s) % count) * width, width, axis=2)
        for s in range(count)
    ]
    grad_sum = sum(
        jnp.einsum(
            "bco,ohw->bchw", pw_slots[s], cot_full[s * width : (s + 1) * width],
            preferred_element_type=jnp.float32,
        )
        for s in range(count)
    )
    grad_branches = grad_sum.astype(jnp.bfloat16)
    requests = {}
    for which, spacing in enumerate(dilations):
        for side in (-1, 1):
            requests[(which, side * spacing)] = (grad_branches[which + 1], side * spacing)
    grad_halo = halo_rows(requests)

    feat_rows = {0: features.astype(jnp.float32)}
    for offset, rows in feat_halo.items():
        feat_rows[offset] = rows.astype(jnp.float32)
    branches = [features]
    for which, spacing in enumerate(dilations):
        total = jnp.zeros(features.shape, jnp.float32)
        for tap_index in range(9):
            row_step = tap_index // 3 - 1
            col_step = tap_index % 3 - 1
            total = total + kernel[which, tap_index][:, None, None] * jnp.roll(
                feat_rows[row_step * spacing], -col_step * spacing, axis=-1
            )
        branches.append(total.astype(jnp.bfloat16))
    stacked = jnp.stack(branches)

    partial = jnp.einsum(
        "bchw,bco->ohw", stacked, pointwise, preferred_element_type=jnp.float32
    ).astype(jnp.bfloat16)
    result = lax.dynamic_slice_in_dim(partial, me * width, width, axis=0).astype(jnp.float32)
    for s in range(1, count):
        piece = lax.dynamic_slice_in_dim(partial, ((me + s) % count) * width, width, axis=0)
        result = result + chan_shift(piece, s).astype(jnp.float32)
    output = result.astype(jnp.bfloat16)

    point_local = jnp.zeros(pointwise.shape, jnp.float32)
    for s in range(count):
        point_slot = jnp.einsum(
            "bchw,ohw->bco", stacked, cot_full[s * width : (s + 1) * width],
            preferred_element_type=jnp.float32,
        )
        point_local = lax.dynamic_update_slice_in_dim(
            point_local, point_slot, ((me - s) % count) * width, axis=2
        )

    depth_rows = []
    for which, spacing in enumerate(dilations):
        grad_f = grad_branches[which + 1].astype(jnp.float32)
        tap_rows = []
        for tap_index in range(9):
            row_step = tap_index // 3 - 1
            col_step = tap_index % 3 - 1
            tap_rows.append(
                jnp.sum(
                    grad_f * jnp.roll(feat_rows[row_step * spacing], -col_step * spacing, axis=-1),
                    axis=(1, 2),
                )
            )
        depth_rows.append(jnp.stack(tap_rows))
    depth_local = jnp.stack(depth_rows)
    flat = jnp.concatenate([depth_local.reshape(-1), point_local.reshape(-1)])
    flat = lax.psum(flat, "band")
    depth_total = flat[: depth_local.size].reshape(depth_local.shape)
    point_total = flat[depth_local.size :].reshape(point_local.shape)

    grad_input = grad_branches[0].astype(jnp.float32)
    for which, spacing in enumerate(dilations):
        grad_rows = {0: grad_branches[which + 1].astype(jnp.float32)}
        for side in (-1, 1):
            grad_rows[side * spacing] = grad_halo[(which, side * spacing)].astype(jnp.float32)
        for tap_index in range(9):
            row_step = tap_index // 3 - 1
            col_step = tap_index % 3 - 1
            grad_input = grad_input + kernel[which, tap_index][:, None, None] * jnp.roll(
                grad_rows[-row_step * spacing], col_step * spacing, axis=-1
            )
    return (output, grad_input, depth_total / GSCALE, point_total / GSCALE)


def solution(mesh):
    return jax.shard_map(
        block,
        mesh=mesh,
        in_specs=(
            P("chan", "band", None),
            P(None, None, "chan"),
            P(None, "chan", None),
            P("chan", "band", None),
        ),
        out_specs=(
            P("chan", "band", None),
            P("chan", "band", None),
            P(None, None, "chan"),
            P(None, "chan", None),
        ),
        check_vma=False,
    )
```

profile of v0, /device:TPU:3, one launch (start us, length us, event | category | flops | bytes accessed | tf_op | source)
XLA Modules:
  0.0 363.8 jit_solution(3913324519702558136)
XLA Ops:
  7.2 2.0 copy.25
  10.2 2.6 collective-permute-start.2
  17.3 8.0 %collective-permute-start.6 = (bf16[128,2,1024]{0,2,1:T(8,128)(2,1)}, bf16[128,2,1024]{0,2,1:T(8,128)(2,1)}, u32[]{:S(2)}, u32[]{:S(2)}) collective-permute-start(bf16[128,2,1024]{0,2,1:T(8,128)(2,1)} %get-tuple-element.121), channel_id=1, source_target_pairs={{0,10},{2,12},{4,14},{6,16},{8,18},{10,20},{12,22},{14,24},{16,26}... | collective-permute-start | bytes 1572872 | tf_op jit(solution)/shard_map/ppermute | solution.py:18
  25.3 2.3 fusion.131
  27.6 2.3 fusion.127
  30.5 2.2 fusion.123
  34.6 2.6 copy.33
  37.2 2.5 fusion.78
  39.8 3.0 collective-permute-start.7
  42.8 23.9 %collective-permute-done.9 = bf16[128,2,1024]{0,2,1:T(8,128)(2,1)} collective-permute-done((bf16[128,2,1024]{0,2,1:T(8,128)(2,1)}, bf16[128,2,1024]{0,2,1:T(8,128)(2,1)}, u32[]{:S(2)}, u32[]{:S(2)}) %collective-permute-start.9) | collective-permute-done | bytes 524320 | tf_op jit(solution)/shard_map/ppermute | solution.py:18
  70.0 2.2 fusion.115
  74.1 5.1 %collective-permute-start.1 = (bf16[128,2,1024]{0,2,1:T(8,128)(2,1)}, bf16[128,2,1024]{0,2,1:T(8,128)(2,1)S(1)}, u32[]{:S(2)}, u32[]{:S(2)}) collective-permute-start(bf16[128,2,1024]{0,2,1:T(8,128)(2,1)} %get-tuple-element.122), channel_id=1, source_target_pairs={{0,2},{2,4},{4,6},{6,8},{8,10},{10,12},{12,14},{14,16},{16,18},{18... | collective-permute-start | bytes 1572872 | tf_op jit(solution)/shard_map/ppermute | solution.py:18
  79.7 2.6 collective-permute-done
  82.3 10.5 %collective-permute-start.4 = (bf16[128,4,1024]{0,2,1:T(8,128)(2,1)S(1)}, bf16[128,4,1024]{0,2,1:T(8,128)(2,1)S(1)}, u32[]{:S(2)}, u32[]{:S(2)}) collective-permute-start(bf16[128,4,1024]{0,2,1:T(8,128)(2,1)S(1)} %copy.25), channel_id=1, source_target_pairs={{0,6},{2,8},{4,10},{6,12},{8,14},{10,16},{12,18},{14,20},{16,22},{... | collective-permute-start | bytes 3145736 | tf_op jit(solution)/shard_map/ppermute | solution.py:18
  97.3 4.6 %fusion.82 = bf16[1,128,4,1024]{1,3,0,2:T(8,128)(2,1)} fusion(f32[128,4,6]{0,2,1:T(8,128)S(1)} %get-tuple-element.78, f32[128,4,1018]{0,2,1:T(8,128)S(1)} %get-tuple-element.80, f32[128]{0:T(128)S(1)} %copy-done.75, f32[128]{0:T(128)S(1)} %copy-done.76, f32[128,4,1018]{0,2,1:T(8,128)S(1)} %get-tuple-element.79, f32[128,4,6]{0,2,1:T(8,128)S(1)} %get-tuple-element.77, ...), kind=kLoop, calls=%fused_computation.170 | loop fusion | flops 15204352 | bytes 16781824 | tf_op jit(solution)/shard_map/stack | solution.py:99
  102.0 2.3 fusion.113
  104.7 7.0 %fusion.80 = bf16[1,128,4,1024]{1,3,0,2:T(8,128)(2,1)} fusion(f32[128,4,18]{0,2,1:T(8,128)S(1)} %get-tuple-element.86, f32[128,4,1006]{0,2,1:T(8,128)} %get-tuple-element.88, f32[128]{0:T(128)S(1)} %copy-done.65, f32[128]{0:T(128)S(1)} %copy-done.66, f32[128,4,1006]{0,2,1:T(8,128)} %get-tuple-element.87, f32[128,4,18]{0,2,1:T(8,128)S(1)} %get-tuple-element.85, ...), kind=kLoop, calls=%fused_computation.168 | loop fusion | flops 15204352 | bytes 16781824 | tf_op jit(solution)/shard_map/stack | solution.py:99
  111.7 3.3 collective-permute-done.11
  115.0 2.5 add_convert_fusion
  117.6 3.2 fusion.93
  121.8 5.3 %collective-permute-start.20 = (bf16[128,2,1024]{0,2,1:T(8,128)(2,1)}, bf16[128,2,1024]{0,2,1:T(8,128)(2,1)}, u32[]{:S(2)}, u32[]{:S(2)}) collective-permute-start(bf16[128,2,1024]{0,2,1:T(8,128)(2,1)} %get-tuple-element.89), channel_id=1, source_target_pairs={{0,10},{2,12},{4,14},{6,16},{8,18},{10,20},{12,22},{14,24},{16,26}... | collective-permute-start | bytes 1572872 | tf_op jit(solution)/shard_map/ppermute | solution.py:18
  128.5 4.8 %collective-permute-start.21 = (bf16[128,2,1024]{0,2,1:T(8,128)(2,1)}, bf16[128,2,1024]{0,2,1:T(8,128)(2,1)}, u32[]{:S(2)}, u32[]{:S(2)}) collective-permute-start(bf16[128,2,1024]{0,2,1:T(8,128)(2,1)} %get-tuple-element.90), channel_id=1, source_target_pairs={{0,8},{2,10},{4,12},{6,14},{8,16},{10,18},{12,20},{14,22},{16,24},... | collective-permute-start | bytes 1572872 | tf_op jit(solution)/shard_map/ppermute | solution.py:18
  136.4 2.2 fusion.101
  138.6 2.3 fusion.105
  141.3 2.0 copy-done.7
  144.7 2.4 fusion.47
  147.1 4.6 %fusion.49 = (f32[128]{0:T(128)}, f32[128]{0:T(128)}, f32[128]{0:T(128)}, f32[128]{0:T(128)}, f32[128]{0:T(128)}, /*index=5*/f32[128]{0:T(128)}) fusion(f32[128,4,6]{0,2,1:T(8,128)S(1)} %copy-done.51, f32[128,4,1018]{0,2,1:T(8,128)S(1)} %get-tuple-element.80, bf16[4,128,4,1024]{1,3,2,0:T(8,128)(2,1)S(1)} %add_convert_fusion, ...), kind=kLoop, calls=%fused_computation.85 | loop fusion | flops 11009280 | bytes 13634560 | tf_op jit(solution)/shard_map/reduce_sum | solution.py:128
  151.8 3.7 %fusion.45 = (f32[128]{0:T(128)}, f32[128]{0:T(128)}, f32[128]{0:T(128)}, f32[128]{0:T(128)}, f32[128]{0:T(128)}, /*index=5*/f32[128]{0:T(128)}, f32[128]{0:T(128)}, f32[128]{0:T(128)}) fusion(bf16[128,4,1024]{0,2,1:T(8,128)(2,1)S(1)} %copy.25, bf16[4,128,4,1024]{1,3,2,0:T(8,128)(2,1)S(1)} %add_convert_fusion, f32[128,4,6]{0,2,1:T(8,128)S(1)} %copy-done.49, ...), kind=kLoop, calls=%fused_computation.81 | loop fusion | flops 13630464 | bytes 13635584 | tf_op jit(solution)/shard_map/reduce_sum | solution.py:128
  155.5 4.3 %fusion.48 = (f32[128]{0:T(128)}, f32[128]{0:T(128)}, f32[128]{0:T(128)}, f32[128]{0:T(128)}, f32[128]{0:T(128)}, /*index=5*/f32[128]{0:T(128)}, f32[128]{0:T(128)}) fusion(bf16[128,2,1024]{0,2,1:T(8,128)(2,1)S(1)} %copy-done.22, bf16[128,2,1024]{0,2,1:T(8,128)(2,1)S(1)} %copy-done.20, bf16[4,128,4,1024]{1,3,2,0:T(8,128)(2,1)S(1)} %add_convert_fusion, ...), kind=kLoop, calls=%fused_computation.84 | loop fusion | flops 13630592 | bytes 13635072 | tf_op jit(solution)/shard_map/reduce_sum | solution.py:128
  161.9 2.5 stack.153
  166.5 5.9 %fusion.81 = bf16[1,128,4,1024]{1,3,0,2:T(8,128)(2,1)S(1)} fusion(f32[128,4,12]{0,2,1:T(8,128)} %copy-done.44, f32[128,4,1012]{0,2,1:T(8,128)} %copy-done.10, f32[128]{0:T(128)} %get-tuple-element.133, bf16[128,4,1024]{0,2,1:T(8,128)(2,1)S(1)} %collective-permute-done.5, f32[128]{0:T(128)} %get-tuple-element.134, f32[128,4,1012]{0,2,1:T(8,128)} %copy-done.9, ...), kind=kLoop, calls=%fused_computation.169 | loop fusion | flops 14155776 | bytes 16781824 | tf_op jit(solution)/shard_map/stack | solution.py:99
  172.4 2.5 bitcast_convert_fusion
  176.7 2.6 fusion.73
  181.5 5.2 %collective-permute-start.14 = (bf16[128,2,1024]{0,2,1:T(8,128)(2,1)}, bf16[128,2,1024]{0,2,1:T(8,128)(2,1)S(1)}, u32[]{:S(2)}, u32[]{:S(2)}) collective-permute-start(bf16[128,2,1024]{0,2,1:T(8,128)(2,1)} %get-tuple-element.99), channel_id=1, source_target_pairs={{0,4},{2,6},{4,8},{6,10},{8,12},{10,14},{12,16},{14,18},{16,20},{1... | collective-permute-start | bytes 1572872 | tf_op jit(solution)/shard_map/ppermute | solution.py:18
  186.8 2.3 fusion.97
  190.5 82.7 %all-reduce.2.cloned.1.call-done = f32[134528]{0:T(1024)} async-done(((f32[134528]{0:T(1024)}), f32[134528]{0:T(1024)}) %all-reduce.2.cloned.1.call-update) | async-done | bytes 538128 | tf_op jit(solution)/shard_map/psum | solution.py:136
  276.6 2.8 collective-permute-start.12
  279.4 4.5 %collective-permute-start.15 = (bf16[128,2,1024]{0,2,1:T(8,128)(2,1)}, bf16[128,2,1024]{0,2,1:T(8,128)(2,1)S(1)}, u32[]{:S(2)}, u32[]{:S(2)}) collective-permute-start(bf16[128,2,1024]{0,2,1:T(8,128)(2,1)} %get-tuple-element.100), channel_id=1, source_target_pairs={{0,2},{2,4},{4,6},{6,8},{8,10},{10,12},{12,14},{14,16},{16,18},{18... | collective-permute-start | bytes 1572872 | tf_op jit(solution)/shard_map/ppermute | solution.py:18
  285.3 1.9 collective-permute-start.13
  287.2 3.0 collective-permute-start.17
  291.6 2.4 fusion.95
  294.0 2.7 collective-permute-start.16
  298.1 2.2 fusion.99
  303.4 25.3 %collective-permute-done.17 = bf16[128,4,1024]{0,2,1:T(8,128)(2,1)S(1)} collective-permute-done((bf16[128,4,1024]{0,2,1:T(8,128)(2,1)S(1)}, bf16[128,4,1024]{0,2,1:T(8,128)(2,1)S(1)}, u32[]{:S(2)}, u32[]{:S(2)}) %collective-permute-start.17) | collective-permute-done | bytes 1048608 | tf_op jit(solution)/shard_map/ppermute | solution.py:18
  328.8 2.3 fusion.118
  331.1 2.4 fusion.120
  336.1 15.4 %fusion.40 = f32[128,4,1024]{0,2,1:T(8,128)S(1)} fusion(f32[128,4,6]{0,2,1:T(8,128)} %get-tuple-element.70, f32[128,4,1018]{0,2,1:T(8,128)S(1)} %get-tuple-element.72, f32[128,4,1018]{0,2,1:T(8,128)S(1)} %get-tuple-element.71, f32[128,4,6]{0,2,1:T(8,128)S(1)} %get-tuple-element.69, f32[128,4,6]{0,2,1:T(8,128)S(1)} %copy-done.61, ...), kind=kLoop, calls=%fused_computation.76 | loop fusion | flops 45088768 | bytes 50345472 | tf_op jit(solution)/shard_map/add | solution.py:148
  351.5 2.0 copy.41
  (250 shorter events, 51.6 us)
Async XLA Ops:
  7.2 30.1 %copy-start = (bf16[4,128,256]{2,1,0:T(8,128)(2,1)S(1)}, bf16[4,128,256]{2,1,0:T(8,128)(2,1)}, u32[]{:S(2)}) copy-start(bf16[4,128,256]{2,1,0:T(8,128)(2,1)} %param.6) | copy-start | bytes 786436
  7.2 266.0 %all-reduce.2.cloned.1.call-start = ((), (), s32[]{:S(2)}) async-start(), calls=%async_computation | async-start | bytes 1081344 | tf_op jit(solution)/shard_map/psum | solution.py:136
  10.2 62.0 %collective-permute-start.2 = (bf16[128,2,1024]{0,2,1:T(8,128)(2,1)}, bf16[128,2,1024]{0,2,1:T(8,128)(2,1)S(1)}, u32[]{:S(2)}, u32[]{:S(2)}) collective-permute-start(bf16[128,2,1024]{0,2,1:T(8,128)(2,1)} %get-tuple-element.121), channel_id=1, source_target_pairs={{2,0},{4,2},{6,4},{8,6},{10,8},{12,10},{14,12},{16,14},{18,16},{20... | collective-permute-start | bytes 1572872 | tf_op jit(solution)/shard_map/ppermute | solution.py:18
  12.8 26.9 %collective-permute-start.8 = (bf16[128,2,1024]{0,2,1:T(8,128)(2,1)}, bf16[128,2,1024]{0,2,1:T(8,128)(2,1)S(1)}, u32[]{:S(2)}, u32[]{:S(2)}) collective-permute-start(bf16[128,2,1024]{0,2,1:T(8,128)(2,1)} %get-tuple-element.121), channel_id=1, source_target_pairs={{8,0},{10,2},{12,4},{14,6},{16,8},{18,10},{20,12},{22,14},{24,16},... | collective-permute-start | bytes 1572872 | tf_op jit(solution)/shard_map/ppermute | solution.py:18
  14.1 60.0 %collective-permute-start.3 = (bf16[128,2,1024]{0,2,1:T(8,128)(2,1)}, bf16[128,2,1024]{0,2,1:T(8,128)(2,1)S(1)}, u32[]{:S(2)}, u32[]{:S(2)}) collective-permute-start(bf16[128,2,1024]{0,2,1:T(8,128)(2,1)} %get-tuple-element.122), channel_id=1, source_target_pairs={{4,0},{6,2},{8,4},{10,6},{12,8},{14,10},{16,12},{18,14},{20,16},{2... | collective-permute-start | bytes 1572872 | tf_op jit(solution)/shard_map/ppermute | solution.py:18
  16.0 50.7 %collective-permute-start.9 = (bf16[128,2,1024]{0,2,1:T(8,128)(2,1)}, bf16[128,2,1024]{0,2,1:T(8,128)(2,1)}, u32[]{:S(2)}, u32[]{:S(2)}) collective-permute-start(bf16[128,2,1024]{0,2,1:T(8,128)(2,1)} %get-tuple-element.122), channel_id=1, source_target_pairs={{10,0},{12,2},{14,4},{16,6},{18,8},{20,10},{22,12},{24,14},{26,16}... | collective-permute-start | bytes 1572872 | tf_op jit(solution)/shard_map/ppermute | solution.py:18
  17.3 77.5 %collective-permute-start.6 = (bf16[128,2,1024]{0,2,1:T(8,128)(2,1)}, bf16[128,2,1024]{0,2,1:T(8,128)(2,1)}, u32[]{:S(2)}, u32[]{:S(2)}) collective-permute-start(bf16[128,2,1024]{0,2,1:T(8,128)(2,1)} %get-tuple-element.121), channel_id=1, source_target_pairs={{0,10},{2,12},{4,14},{6,16},{8,18},{10,20},{12,22},{14,24},{16,26}... | collective-permute-start | bytes 1572872 | tf_op jit(solution)/shard_map/ppermute | solution.py:18
  39.8 55.1 %collective-permute-start.7 = (bf16[128,2,1024]{0,2,1:T(8,128)(2,1)}, bf16[128,2,1024]{0,2,1:T(8,128)(2,1)S(1)}, u32[]{:S(2)}, u32[]{:S(2)}) collective-permute-start(bf16[128,2,1024]{0,2,1:T(8,128)(2,1)} %get-tuple-element.122), channel_id=1, source_target_pairs={{0,8},{2,10},{4,12},{6,14},{8,16},{10,18},{12,20},{14,22},{16,24},... | collective-permute-start | bytes 1572872 | tf_op jit(solution)/shard_map/ppermute | solution.py:18
  66.7 66.6 %collective-permute-start.5 = (bf16[128,4,1024]{0,2,1:T(8,128)(2,1)S(1)}, bf16[128,4,1024]{0,2,1:T(8,128)(2,1)S(1)}, u32[]{:S(2)}, u32[]{:S(2)}) collective-permute-start(bf16[128,4,1024]{0,2,1:T(8,128)(2,1)S(1)} %copy.25), channel_id=1, source_target_pairs={{6,0},{8,2},{10,4},{12,6},{14,8},{16,10},{18,12},{20,14},{22,16},{... | collective-permute-start | bytes 3145736 | tf_op jit(solution)/shard_map/ppermute | solution.py:18
  72.2 7.5 %copy-start.19 = (bf16[128,2,1024]{0,2,1:T(8,128)(2,1)}, bf16[128,2,1024]{0,2,1:T(8,128)(2,1)S(1)}, u32[]{:S(2)}) copy-start(bf16[128,2,1024]{0,2,1:T(8,128)(2,1)S(1)} %collective-permute-done.2) | copy-start | bytes 1572868
  72.2 10.1 %collective-permute-start = (bf16[128,2,1024]{0,2,1:T(8,128)(2,1)}, bf16[128,2,1024]{0,2,1:T(8,128)(2,1)S(1)}, u32[]{:S(2)}, u32[]{:S(2)}) collective-permute-start(bf16[128,2,1024]{0,2,1:T(8,128)(2,1)} %get-tuple-element.121), channel_id=1, source_target_pairs={{0,4},{2,6},{4,8},{6,10},{8,12},{10,14},{12,16},{14,18},{16,20},{1... | collective-permute-start | bytes 1572872 | tf_op jit(solution)/shard_map/ppermute | solution.py:18
  74.1 5.6 %copy-start.21 = (bf16[128,2,1024]{0,2,1:T(8,128)(2,1)}, bf16[128,2,1024]{0,2,1:T(8,128)(2,1)S(1)}, u32[]{:S(2)}) copy-start(bf16[128,2,1024]{0,2,1:T(8,128)(2,1)S(1)} %collective-permute-done.3) | copy-start | bytes 1572868
  74.1 18.7 %collective-permute-start.1 = (bf16[128,2,1024]{0,2,1:T(8,128)(2,1)}, bf16[128,2,1024]{0,2,1:T(8,128)(2,1)S(1)}, u32[]{:S(2)}, u32[]{:S(2)}) collective-permute-start(bf16[128,2,1024]{0,2,1:T(8,128)(2,1)} %get-tuple-element.122), channel_id=1, source_target_pairs={{0,2},{2,4},{4,6},{6,8},{8,10},{10,12},{12,14},{14,16},{16,18},{18... | collective-permute-start | bytes 1572872 | tf_op jit(solution)/shard_map/ppermute | solution.py:18
  79.4 17.1 %copy-start.50 = (f32[128,4,6]{0,2,1:T(8,128)}, f32[128,4,6]{0,2,1:T(8,128)S(1)}, u32[]{:S(2)}) copy-start(f32[128,4,6]{0,2,1:T(8,128)S(1)} %get-tuple-element.78) | copy-start | bytes 36868
  79.4 17.1 %copy-start.56 = (f32[128,4,6]{0,2,1:T(8,128)}, f32[128,4,6]{0,2,1:T(8,128)S(1)}, u32[]{:S(2)}) copy-start(f32[128,4,6]{0,2,1:T(8,128)S(1)} %get-tuple-element.77) | copy-start | bytes 36868
  82.3 14.2 %copy-start.27 = (bf16[128,2,1024]{0,2,1:T(8,128)(2,1)}, bf16[128,2,1024]{0,2,1:T(8,128)(2,1)S(1)}, u32[]{:S(2)}) copy-start(bf16[128,2,1024]{0,2,1:T(8,128)(2,1)S(1)} %collective-permute-done) | copy-start | bytes 1572868
  82.3 58.6 %collective-permute-start.4 = (bf16[128,4,1024]{0,2,1:T(8,128)(2,1)S(1)}, bf16[128,4,1024]{0,2,1:T(8,128)(2,1)S(1)}, u32[]{:S(2)}, u32[]{:S(2)}) collective-permute-start(bf16[128,4,1024]{0,2,1:T(8,128)(2,1)S(1)} %copy.25), channel_id=1, source_target_pairs={{0,6},{2,8},{4,10},{6,12},{8,14},{10,16},{12,18},{14,20},{16,22},{... | collective-permute-start | bytes 3145736 | tf_op jit(solution)/shard_map/ppermute | solution.py:18
  92.9 22.1 %collective-permute-start.11 = (bf16[128,4,1024]{2,0,1:T(8,128)(2,1)}, bf16[128,4,1024]{2,0,1:T(8,128)(2,1)}, u32[]{:S(2)}, u32[]{:S(2)}) collective-permute-start(bf16[128,4,1024]{2,0,1:T(8,128)(2,1)} %copy.33), channel_id=1, source_target_pairs={{0,1},{1,0},{2,3},{3,2},{4,5},{5,4},{6,7},{7,6},{8,9},{9,8},{10,11... | collective-permute-start | bytes 3145736 | tf_op jit(solution)/shard_map/ppermute | solution.py:52
  117.6 37.8 %copy-start.2 = (bf16[4,128,4,1024]{1,3,2,0:T(8,128)(2,1)}, bf16[4,128,4,1024]{1,3,2,0:T(8,128)(2,1)S(1)}, u32[]{:S(2)}) copy-start(bf16[4,128,4,1024]{1,3,2,0:T(8,128)(2,1)S(1)} %add_convert_fusion) | copy-start | bytes 12582916
  121.8 154.7 %collective-permute-start.20 = (bf16[128,2,1024]{0,2,1:T(8,128)(2,1)}, bf16[128,2,1024]{0,2,1:T(8,128)(2,1)}, u32[]{:S(2)}, u32[]{:S(2)}) collective-permute-start(bf16[128,2,1024]{0,2,1:T(8,128)(2,1)} %get-tuple-element.89), channel_id=1, source_target_pairs={{0,10},{2,12},{4,14},{6,16},{8,18},{10,20},{12,22},{14,24},{16,26}... | collective-permute-start | bytes 1572872 | tf_op jit(solution)/shard_map/ppermute | solution.py:18
  127.2 158.1 %collective-permute-start.18 = (bf16[128,2,1024]{0,2,1:T(8,128)(2,1)}, bf16[128,2,1024]{0,2,1:T(8,128)(2,1)}, u32[]{:S(2)}, u32[]{:S(2)}) collective-permute-start(bf16[128,2,1024]{0,2,1:T(8,128)(2,1)} %get-tuple-element.89), channel_id=1, source_target_pairs={{8,0},{10,2},{12,4},{14,6},{16,8},{18,10},{20,12},{22,14},{24,16},... | collective-permute-start | bytes 1572872 | tf_op jit(solution)/shard_map/ppermute | solution.py:18
  128.5 150.9 %collective-permute-start.21 = (bf16[128,2,1024]{0,2,1:T(8,128)(2,1)}, bf16[128,2,1024]{0,2,1:T(8,128)(2,1)}, u32[]{:S(2)}, u32[]{:S(2)}) collective-permute-start(bf16[128,2,1024]{0,2,1:T(8,128)(2,1)} %get-tuple-element.90), channel_id=1, source_target_pairs={{0,8},{2,10},{4,12},{6,14},{8,16},{10,18},{12,20},{14,22},{16,24},... | collective-permute-start | bytes 1572872 | tf_op jit(solution)/shard_map/ppermute | solution.py:18
  133.3 153.9 %collective-permute-start.19 = (bf16[128,2,1024]{0,2,1:T(8,128)(2,1)}, bf16[128,2,1024]{0,2,1:T(8,128)(2,1)}, u32[]{:S(2)}, u32[]{:S(2)}) collective-permute-start(bf16[128,2,1024]{0,2,1:T(8,128)(2,1)} %get-tuple-element.90), channel_id=1, source_target_pairs={{10,0},{12,2},{14,4},{16,6},{18,8},{20,10},{22,12},{24,14},{26,16}... | collective-permute-start | bytes 1572872 | tf_op jit(solution)/shard_map/ppermute | solution.py:18
  135.1 6.2 %copy-start.9 = (f32[128,4,1012]{0,2,1:T(8,128)}, f32[128,4,1012]{0,2,1:T(8,128)S(1)}, u32[]{:S(2)}) copy-start(f32[128,4,1012]{0,2,1:T(8,128)S(1)} %get-tuple-element.115) | copy-start | bytes 6217732
  135.1 20.3 %copy-start.10 = (f32[128,4,1012]{0,2,1:T(8,128)}, f32[128,4,1012]{0,2,1:T(8,128)S(1)}, u32[]{:S(2)}) copy-start(f32[128,4,1012]{0,2,1:T(8,128)S(1)} %get-tuple-element.116) | copy-start | bytes 6217732
  135.1 6.2 %copy-start.42 = (f32[128,4,12]{0,2,1:T(8,128)}, f32[128,4,12]{0,2,1:T(8,128)S(1)}, u32[]{:S(2)}) copy-start(f32[128,4,12]{0,2,1:T(8,128)S(1)} %get-tuple-element.113) | copy-start | bytes 73732
  135.1 20.3 %copy-start.44 = (f32[128,4,12]{0,2,1:T(8,128)}, f32[128,4,12]{0,2,1:T(8,128)S(1)}, u32[]{:S(2)}) copy-start(f32[128,4,12]{0,2,1:T(8,128)S(1)} %get-tuple-element.114) | copy-start | bytes 73732
  141.2 5.8 %copy-start.11 = (f32[128,4,1012]{0,2,1:T(8,128)}, f32[128,4,1012]{0,2,1:T(8,128)S(1)}, u32[]{:S(2)}) copy-start(f32[128,4,1012]{0,2,1:T(8,128)S(1)} %get-tuple-element.107) | copy-start | bytes 6217732
  141.2 5.8 %copy-start.12 = (f32[128,4,1012]{0,2,1:T(8,128)}, f32[128,4,1012]{0,2,1:T(8,128)S(1)}, u32[]{:S(2)}) copy-start(f32[128,4,1012]{0,2,1:T(8,128)S(1)} %get-tuple-element.108) | copy-start | bytes 6217732
  141.2 5.8 %copy-start.45 = (f32[128,4,12]{0,2,1:T(8,128)}, f32[128,4,12]{0,2,1:T(8,128)S(1)}, u32[]{:S(2)}) copy-start(f32[128,4,12]{0,2,1:T(8,128)S(1)} %get-tuple-element.105) | copy-start | bytes 73732
  141.3 5.8 %copy-start.47 = (f32[128,4,12]{0,2,1:T(8,128)}, f32[128,4,12]{0,2,1:T(8,128)S(1)}, u32[]{:S(2)}) copy-start(f32[128,4,12]{0,2,1:T(8,128)S(1)} %get-tuple-element.106) | copy-start | bytes 73732
  155.5 11.0 %copy-start.41 = (f32[128,4,12]{0,2,1:T(8,128)S(1)}, f32[128,4,12]{0,2,1:T(8,128)}, u32[]{:S(2)}) copy-start(f32[128,4,12]{0,2,1:T(8,128)} %get-tuple-element.110) | copy-start | bytes 73732
  155.5 11.0 %copy-start.43 = (f32[128,4,12]{0,2,1:T(8,128)S(1)}, f32[128,4,12]{0,2,1:T(8,128)}, u32[]{:S(2)}) copy-start(f32[128,4,12]{0,2,1:T(8,128)} %copy-done.42) | copy-start | bytes 73732
  155.5 11.0 %copy-start.46 = (f32[128,4,12]{0,2,1:T(8,128)S(1)}, f32[128,4,12]{0,2,1:T(8,128)}, u32[]{:S(2)}) copy-start(f32[128,4,12]{0,2,1:T(8,128)} %copy-done.45) | copy-start | bytes 73732
  166.4 5.9 %copy-start.37 = (bf16[1,128,4,1024]{1,3,0,2:T(8,128)(2,1)S(1)}, bf16[1,128,4,1024]{1,3,0,2:T(8,128)(2,1)}, u32[]{:S(2)}) copy-start(bf16[1,128,4,1024]{1,3,0,2:T(8,128)(2,1)} %fusion.82) | copy-start | bytes 3145732
  166.5 5.9 %copy-start.38 = (bf16[1,128,4,1024]{1,3,0,2:T(8,128)(2,1)S(1)}, bf16[1,128,4,1024]{1,3,0,2:T(8,128)(2,1)}, u32[]{:S(2)}) copy-start(bf16[1,128,4,1024]{1,3,0,2:T(8,128)(2,1)} %fusion.80) | copy-start | bytes 3145732
  179.5 7.3 %copy-start.4 = (f32[128,4,1024]{0,2,1:T(8,128)S(1)}, f32[128,4,1024]{0,2,1:T(8,128)}, u32[]{:S(2)}) copy-start(f32[128,4,1024]{0,2,1:T(8,128)} %get-tuple-element.39) | copy-start | bytes 6291460
  181.5 112.4 %collective-permute-start.14 = (bf16[128,2,1024]{0,2,1:T(8,128)(2,1)}, bf16[128,2,1024]{0,2,1:T(8,128)(2,1)S(1)}, u32[]{:S(2)}, u32[]{:S(2)}) collective-permute-start(bf16[128,2,1024]{0,2,1:T(8,128)(2,1)} %get-tuple-element.99), channel_id=1, source_target_pairs={{0,4},{2,6},{4,8},{6,10},{8,12},{10,14},{12,16},{14,18},{16,20},{1... | collective-permute-start | bytes 1572872 | tf_op jit(solution)/shard_map/ppermute | solution.py:18
  274.3 11.0 %copy-start.39 = (bf16[128,2,1024]{0,2,1:T(8,128)(2,1)S(1)}, bf16[128,2,1024]{0,2,1:T(8,128)(2,1)}, u32[]{:S(2)}) copy-start(bf16[128,2,1024]{0,2,1:T(8,128)(2,1)} %get-tuple-element.100) | copy-start | bytes 1572868
  274.3 12.9 %copy-start.36 = (bf16[128,4,1024]{0,2,1:T(8,128)(2,1)S(1)}, bf16[128,4,1024]{0,2,1:T(8,128)(2,1)}, u32[]{:S(2)}) copy-start(bf16[128,4,1024]{0,2,1:T(8,128)(2,1)} %get-tuple-element.43) | copy-start | bytes 3145732
  276.6 23.7 %collective-permute-start.12 = (bf16[128,2,1024]{0,2,1:T(8,128)(2,1)}, bf16[128,2,1024]{0,2,1:T(8,128)(2,1)S(1)}, u32[]{:S(2)}, u32[]{:S(2)}) collective-permute-start(bf16[128,2,1024]{0,2,1:T(8,128)(2,1)} %get-tuple-element.99), channel_id=1, source_target_pairs={{2,0},{4,2},{6,4},{8,6},{10,8},{12,10},{14,12},{16,14},{18,16},{20... | collective-permute-start | bytes 1572872 | tf_op jit(solution)/shard_map/ppermute | solution.py:18
  279.4 17.2 %collective-permute-start.15 = (bf16[128,2,1024]{0,2,1:T(8,128)(2,1)}, bf16[128,2,1024]{0,2,1:T(8,128)(2,1)S(1)}, u32[]{:S(2)}, u32[]{:S(2)}) collective-permute-start(bf16[128,2,1024]{0,2,1:T(8,128)(2,1)} %get-tuple-element.100), channel_id=1, source_target_pairs={{0,2},{2,4},{4,6},{6,8},{8,10},{10,12},{12,14},{14,16},{16,18},{18... | collective-permute-start | bytes 1572872 | tf_op jit(solution)/shard_map/ppermute | solution.py:18
  285.3 16.4 %collective-permute-start.13 = (bf16[128,2,1024]{0,2,1:T(8,128)(2,1)S(1)}, bf16[128,2,1024]{0,2,1:T(8,128)(2,1)S(1)}, u32[]{:S(2)}, u32[]{:S(2)}) collective-permute-start(bf16[128,2,1024]{0,2,1:T(8,128)(2,1)S(1)} %copy-done.39), channel_id=1, source_target_pairs={{4,0},{6,2},{8,4},{10,6},{12,8},{14,10},{16,12},{18,14},{20,16},{2... | collective-permute-start | bytes 1572872 | tf_op jit(solution)/shard_map/ppermute | solution.py:18
  287.2 41.5 %collective-permute-start.17 = (bf16[128,4,1024]{0,2,1:T(8,128)(2,1)S(1)}, bf16[128,4,1024]{0,2,1:T(8,128)(2,1)S(1)}, u32[]{:S(2)}, u32[]{:S(2)}) collective-permute-start(bf16[128,4,1024]{0,2,1:T(8,128)(2,1)S(1)} %copy-done.36), channel_id=1, source_target_pairs={{0,6},{2,8},{4,10},{6,12},{8,14},{10,16},{12,18},{14,20},{16,22},{... | collective-permute-start | bytes 3145736 | tf_op jit(solution)/shard_map/ppermute | solution.py:18
  294.0 37.1 %collective-permute-start.16 = (bf16[128,4,1024]{0,2,1:T(8,128)(2,1)S(1)}, bf16[128,4,1024]{0,2,1:T(8,128)(2,1)S(1)}, u32[]{:S(2)}, u32[]{:S(2)}) collective-permute-start(bf16[128,4,1024]{0,2,1:T(8,128)(2,1)S(1)} %copy-done.36), channel_id=1, source_target_pairs={{6,0},{8,2},{10,4},{12,6},{14,8},{16,10},{18,12},{20,14},{22,16},{... | collective-permute-start | bytes 3145736 | tf_op jit(solution)/shard_map/ppermute | solution.py:18
  296.6 56.8 %collective-permute-start.10 = (bf16[128,4,1024]{0,2,1:T(8,128)(2,1)}, bf16[128,4,1024]{0,2,1:T(8,128)(2,1)}, u32[]{:S(2)}, u32[]{:S(2)}) collective-permute-start(bf16[128,4,1024]{0,2,1:T(8,128)(2,1)} %dynamic-slice_bitcast_fusion), channel_id=1, source_target_pairs={{0,1},{1,0},{2,3},{3,2},{4,5},{5,4},{6,7},{7,6},{8,9},{9,8},{10,11... | collective-permute-start | bytes 3145736 | tf_op jit(solution)/shard_map/ppermute | solution.py:52
  331.1 5.0 %copy-start.3 = (bf16[4,128,4,1024]{1,3,2,0:T(8,128)(2,1)S(1)}, bf16[4,128,4,1024]{1,3,2,0:T(8,128)(2,1)}, u32[]{:S(2)}) copy-start(bf16[4,128,4,1024]{1,3,2,0:T(8,128)(2,1)} %copy-done.2) | copy-start | bytes 12582916
  351.4 5.5 %copy-start.1 = (bf16[4,128,256]{2,1,0:T(8,128)(2,1)S(1)}, bf16[4,128,256]{2,1,0:T(8,128)(2,1)}, u32[]{:S(2)}) copy-start(bf16[4,128,256]{2,1,0:T(8,128)(2,1)} %param.6) | copy-start | bytes 786436
  (59 other events, 176.1 us)
Sparse Core Ops, SparseCore 0:
  180.5 92.6 all-reduce.1
where the time goes:
time: 365 us; the launch traced here: 364 us
  waiting for transfers between devices  139 us (38%)
  starting transfers between devices  73.1 us (20%)
  other arithmetic  63 us (17%)
  local copies, waits for them, and re-layouts  61.1 us (17%)
  between operations  15.4 us (4%)
  matrix products  11.8 us (3%)
    psum x1, waiting for transfers between devices, block(): flat = lax.psum(flat, 'band')  82.7 us
    ppermute x20, starting transfers between devices, shifted(): return lax.ppermute(block, axis, route)  70.5 us
    ppermute x20, waiting for transfers between devices, shifted(): return lax.ppermute(block, axis, route)  53.3 us
    slice x18, local copies, waits for them, and re-layouts, block(): jnp.roll(grad_rows[-row_step * spacing], col_step * spacing, axis=-1)  18.6 us
    another operation x3, other arithmetic, block(): stacked = jnp.stack(branches)  17.5 us
    unnamed x174, local copies, waits for them, and re-layouts  16.9 us
    add x1, other arithmetic, block(): grad_input + kernel[which, tap_index][:, None, None] * jnp.roll(grad_rows...  15.4 us
    reduce_sum x4, other arithmetic, block(): jnp.sum(grad_f * jnp.roll(feat_rows[row_step * spacing], -col_step * spac...  14.9 us
  transfers between devices with their start and end apart: 23, of which 6 were waited for; matrix products, arithmetic and copies ran while one was open for 33% of the time, Pallas kernels for 0%

commit v1 on v0

--- a/solution.py
+++ b/solution.py
@@ -45,6 +45,54 @@
         parts = got[key]
         out[key] = parts[0][1] if len(parts) == 1 else jnp.concatenate([p for _, p in parts], axis=1)
     return out
+
+
+def band_allreduce(flat):
+    count = lax.axis_size("band")
+    radices = []
+    rest = count
+    while rest % 4 == 0:
+        radices.append(4)
+        rest //= 4
+    while rest % 2 == 0:
+        radices.append(2)
+        rest //= 2
+    if rest != 1:
+        return lax.psum(flat, "band")
+    length = flat.shape[0]
+    flat = jnp.pad(flat, (0, (-length) % count))
+    me = lax.axis_index("band")
+    steps = []
+    stride = 1
+    for radix in radices:
+        steps.append((stride, radix))
+        stride *= radix
+
+    def rotate(stride, radix, u):
+        return [
+            (j, j + (((j // stride) % radix + u) % radix - (j // stride) % radix) * stride)
+            for j in range(count)
+        ]
+
+    for stride, radix in steps:
+        digit = (me // stride) % radix
+        size = flat.shape[0] // radix
+        acc = lax.dynamic_slice_in_dim(flat, digit * size, size)
+        for u in range(1, radix):
+            give = lax.dynamic_slice_in_dim(flat, ((digit + u) % radix) * size, size)
+            acc = acc + lax.ppermute(give, "band", rotate(stride, radix, u))
+        flat = acc
+    for stride, radix in reversed(steps):
+        digit = (me // stride) % radix
+        size = flat.shape[0]
+        full = lax.dynamic_update_slice_in_dim(
+            jnp.zeros((size * radix,), flat.dtype), flat, digit * size, 0
+        )
+        for u in range(1, radix):
+            got = lax.ppermute(flat, "band", rotate(stride, radix, u))
+            full = lax.dynamic_update_slice_in_dim(full, got, ((digit - u) % radix) * size, 0)
+        flat = full
+    return flat[:length]
 
 
 def chan_shift(block, s):
@@ -133,7 +181,7 @@
         depth_rows.append(jnp.stack(tap_rows))
     depth_local = jnp.stack(depth_rows)
     flat = jnp.concatenate([depth_local.reshape(-1), point_local.reshape(-1)])
-    flat = lax.psum(flat, "band")
+    flat = band_allreduce(flat)
     depth_total = flat[: depth_local.size].reshape(depth_local.shape)
     point_total = flat[depth_local.size :].reshape(point_local.shape)
 

time: 365 us -> 317 us (0.87)
  the two profiles are of different devices: /device:TPU:3 before, /device:TPU:12 now
where the time goes in v1:
time: 317 us; the launch traced here: 311 us
  starting transfers between devices  90.9 us (29%)
  local copies, waits for them, and re-layouts  74.8 us (24%)
  waiting for transfers between devices  68 us (21%)
  other arithmetic  62.8 us (20%)
  matrix products  12 us (4%)
    ppermute x20, starting transfers between devices, shifted(): return lax.ppermute(block, axis, route)  67.4 us
    ppermute x20, waiting for transfers between devices, shifted(): return lax.ppermute(block, axis, route)  39.9 us
    slice x18, local copies, waits for them, and re-layouts, block(): jnp.roll(grad_rows[-row_step * spacing], col_step * spacing, axis=-1)  23.6 us
    unnamed x223, local copies, waits for them, and re-layouts  21.3 us
    reduce_sum x4, other arithmetic, block(): jnp.sum(grad_f * jnp.roll(feat_rows[row_step * spacing], -col_step * spac...  17.3 us
    add x1, other arithmetic, block(): grad_input + kernel[which, tap_index][:, None, None] * jnp.roll(grad_rows...  16.5 us
    ppermute x2, waiting for transfers between devices, chan_shift(): lax.ppermute(block, 'chan', [(j, (j + s) % count) for j in range(count)])  16.1 us
    another operation x3, other arithmetic, block(): stacked = jnp.stack(branches)  15.2 us
  transfers between devices with their start and end apart: 34, of which 8 were waited for; matrix products, arithmetic and copies ran while one was open for 26% of the time, Pallas kernels for 0%

profile of v1, /device:TPU:12, one launch (start us, length us, event | category | flops | bytes accessed | tf_op | source)
XLA Modules:
  0.0 311.3 jit_solution(1592572573723628863)
XLA Ops:
  3.7 2.3 collective-permute-start.8
  6.0 3.5 %collective-permute-start.6 = (bf16[128,2,1024]{0,2,1:T(8,128)(2,1)}, bf16[128,2,1024]{0,2,1:T(8,128)(2,1)}, u32[]{:S(2)}, u32[]{:S(2)}) collective-permute-start(bf16[128,2,1024]{0,2,1:T(8,128)(2,1)} %get-tuple-element.123), channel_id=1, source_target_pairs={{0,10},{2,12},{4,14},{6,16},{8,18},{10,20},{12,22},{14,24},{16,26}... | collective-permute-start | bytes 1572872 | tf_op jit(solution)/shard_map/ppermute | solution.py:18
  9.5 4.8 %collective-permute-start.2 = (bf16[128,2,1024]{0,2,1:T(8,128)(2,1)}, bf16[128,2,1024]{0,2,1:T(8,128)(2,1)}, u32[]{:S(2)}, u32[]{:S(2)}) collective-permute-start(bf16[128,2,1024]{0,2,1:T(8,128)(2,1)} %get-tuple-element.123), channel_id=1, source_target_pairs={{2,0},{4,2},{6,4},{8,6},{10,8},{12,10},{14,12},{16,14},{18,16},{20... | collective-permute-start | bytes 1572872 | tf_op jit(solution)/shard_map/ppermute | solution.py:18
  16.2 4.1 %collective-permute-start.7 = (bf16[128,2,1024]{0,2,1:T(8,128)(2,1)}, bf16[128,2,1024]{0,2,1:T(8,128)(2,1)}, u32[]{:S(2)}, u32[]{:S(2)}) collective-permute-start(bf16[128,2,1024]{0,2,1:T(8,128)(2,1)} %get-tuple-element.124), channel_id=1, source_target_pairs={{0,8},{2,10},{4,12},{6,14},{8,16},{10,18},{12,20},{14,22},{16,24},... | collective-permute-start | bytes 1572872 | tf_op jit(solution)/shard_map/ppermute | solution.py:18
  21.6 2.2 fusion.132
  23.7 2.2 fusion.128
  29.0 2.6 copy.33
  31.5 2.5 fusion.78
  35.4 10.4 %collective-permute-start.3 = (bf16[128,2,1024]{0,2,1:T(8,128)(2,1)}, bf16[128,2,1024]{0,2,1:T(8,128)(2,1)S(1)}, u32[]{:S(2)}, u32[]{:S(2)}) collective-permute-start(bf16[128,2,1024]{0,2,1:T(8,128)(2,1)} %get-tuple-element.124), channel_id=1, source_target_pairs={{4,0},{6,2},{8,4},{10,6},{12,8},{14,10},{16,12},{18,14},{20,16},{2... | collective-permute-start | bytes 1572872 | tf_op jit(solution)/shard_map/ppermute | solution.py:18
  47.1 2.3 fusion.114
  49.4 3.0 collective-permute-start.1
  52.4 3.0 collective-permute-done.9
  58.9 6.4 %collective-permute-start.4 = (bf16[128,4,1024]{0,2,1:T(8,128)(2,1)S(1)}, bf16[128,4,1024]{0,2,1:T(8,128)(2,1)S(1)}, u32[]{:S(2)}, u32[]{:S(2)}) collective-permute-start(bf16[128,4,1024]{0,2,1:T(8,128)(2,1)S(1)} %copy.25), channel_id=1, source_target_pairs={{0,6},{2,8},{4,10},{6,12},{8,14},{10,16},{12,18},{14,20},{16,22},{... | collective-permute-start | bytes 3145736 | tf_op jit(solution)/shard_map/ppermute | solution.py:18
  65.2 6.5 %collective-permute-done.3 = bf16[128,2,1024]{0,2,1:T(8,128)(2,1)S(1)} collective-permute-done((bf16[128,2,1024]{0,2,1:T(8,128)(2,1)}, bf16[128,2,1024]{0,2,1:T(8,128)(2,1)S(1)}, u32[]{:S(2)}, u32[]{:S(2)}) %collective-permute-start.3) | collective-permute-done | bytes 524320 | tf_op jit(solution)/shard_map/ppermute | solution.py:18
  76.6 6.1 %fusion.80 = bf16[1,128,4,1024]{1,3,0,2:T(8,128)(2,1)} fusion(f32[128,4,18]{0,2,1:T(8,128)S(1)} %get-tuple-element.88, f32[128,4,1006]{0,2,1:T(8,128)S(1)} %get-tuple-element.90, f32[128]{0:T(128)S(1)} %copy-done.61, f32[128]{0:T(128)S(1)} %copy-done.63, f32[128,4,1006]{0,2,1:T(8,128)S(1)} %get-tuple-element.89, f32[128,4,18]{0,2,1:T(8,128)S(1)} %get-tuple-element.87, ...), kind=kLoop, calls=%fused_computation.168 | loop fusion | flops 15204352 | bytes 16781824 | tf_op jit(solution)/shard_map/stack | solution.py:147
  84.4 5.5 %fusion.82 = bf16[1,128,4,1024]{1,3,0,2:T(8,128)(2,1)} fusion(f32[128,4,6]{0,2,1:T(8,128)S(1)} %get-tuple-element.80, f32[128,4,1018]{0,2,1:T(8,128)S(1)} %get-tuple-element.82, f32[128]{0:T(128)S(1)} %copy-done.87, f32[128]{0:T(128)S(1)} %copy-done.88, f32[128,4,1018]{0,2,1:T(8,128)S(1)} %get-tuple-element.81, f32[128,4,6]{0,2,1:T(8,128)S(1)} %get-tuple-element.79, ...), kind=kLoop, calls=%fused_computation.170 | loop fusion | flops 15204352 | bytes 16781824 | tf_op jit(solution)/shard_map/stack | solution.py:147
  90.0 6.9 %collective-permute-done.11 = bf16[128,4,1024]{2,0,1:T(8,128)(2,1)} collective-permute-done((bf16[128,4,1024]{2,0,1:T(8,128)(2,1)}, bf16[128,4,1024]{2,0,1:T(8,128)(2,1)}, u32[]{:S(2)}, u32[]{:S(2)}) %collective-permute-start.11) | collective-permute-done | bytes 1048608 | tf_op jit(solution)/shard_map/ppermute | solution.py:100
  96.9 2.5 add_convert_fusion
  99.4 3.7 %fusion.93 = (f32[128,4,1024]{0,2,1:T(8,128)S(1)}, f32[128,4,1024]{0,2,1:T(8,128)}, f32[128,4,1024]{0,2,1:T(8,128)S(1)}, bf16[128,4,1024]{0,2,1:T(8,128)(2,1)}, ...) fusion(bf16[4,128,4,1024]{1,3,2,0:T(8,128)(2,1)S(1)} %add_convert_fusion), kind=kLoop, calls=%fused_computation.215 | loop fusion | flops 1572864 | bytes 12582912 | tf_op jit(solution)/shard_map/convert_element_type | solution.py:190
  104.1 2.3 fusion.98
  109.5 2.4 fusion.47
  112.0 3.6 %fusion.81 = bf16[1,128,4,1024]{1,3,0,2:T(8,128)(2,1)S(1)} fusion(f32[128,4,12]{0,2,1:T(8,128)S(1)} %get-tuple-element.116, f32[128,4,1012]{0,2,1:T(8,128)S(1)} %get-tuple-element.118, f32[128]{0:T(128)S(1)} %copy-done.77, bf16[128,4,1024]{0,2,1:T(8,128)(2,1)S(1)} %collective-permute-done.5, f32[128]{0:T(128)S(1)} %copy-done.78, ...), kind=kLoop, calls=%fused_computation.169 | loop fusion | flops 14155776 | bytes 16781824 | tf_op jit(solution)/shard_map/stack | solution.py:147
  115.6 2.6 bitcast_convert_fusion
  120.0 2.7 fusion.73
  123.7 4.7 %fusion.45 = (f32[128]{0:T(128)}, f32[128]{0:T(128)}, f32[128]{0:T(128)}, f32[128]{0:T(128)}, f32[128]{0:T(128)}, /*index=5*/f32[128]{0:T(128)}, f32[128]{0:T(128)}, f32[128]{0:T(128)}) fusion(bf16[128,4,1024]{0,2,1:T(8,128)(2,1)S(1)} %copy.25, bf16[4,128,4,1024]{1,3,2,0:T(8,128)(2,1)S(1)} %add_convert_fusion, f32[128,4,6]{0,2,1:T(8,128)S(1)} %copy-done.48, ...), kind=kLoop, calls=%fused_computation.81 | loop fusion | flops 13630464 | bytes 13635584 | tf_op jit(solution)/shard_map/reduce_sum | solution.py:176
  128.6 3.9 %fusion.48 = (f32[128]{0:T(128)S(1)}, f32[128]{0:T(128)S(1)}, f32[128]{0:T(128)S(1)}, f32[128]{0:T(128)S(1)}, f32[128]{0:T(128)S(1)}, /*index=5*/f32[128]{0:T(128)S(1)}, f32[128]{0:T(128)S(1)}) fusion(bf16[128,2,1024]{0,2,1:T(8,128)(2,1)S(1)} %collective-permute-done.3, bf16[128,2,1024]{0,2,1:T(8,128)(2,1)} %collective-permute-done.2, ...), kind=kLoop, calls=%fused_computation.84 | loop fusion | flops 13630592 | bytes 13635072 | tf_op jit(solution)/shard_map/reduce_sum | solution.py:176
  132.7 6.2 %fusion.49 = (f32[128]{0:T(128)S(1)}, f32[128]{0:T(128)S(1)}, f32[128]{0:T(128)S(1)}, f32[128]{0:T(128)S(1)}, f32[128]{0:T(128)S(1)}, /*index=5*/f32[128]{0:T(128)S(1)}) fusion(f32[128,4,6]{0,2,1:T(8,128)S(1)} %copy-done.50, f32[128,4,1018]{0,2,1:T(8,128)} %copy-done.8, bf16[4,128,4,1024]{1,3,2,0:T(8,128)(2,1)} %copy-done.2, ...), kind=kLoop, calls=%fused_computation.85 | loop fusion | flops 11009280 | bytes 13634560 | tf_op jit(solution)/shard_map/reduce_sum | solution.py:176
  143.9 6.6 %collective-permute-start.22 = (f32[33632]{0:T(1024)S(1)}, f32[33632]{0:T(1024)S(1)}, u32[]{:S(2)}, u32[]{:S(2)}) collective-permute-start(f32[33632]{0:T(1024)S(1)} %get-tuple-element.125), channel_id=1, source_target_pairs={{0,2},{2,4},{4,6},{6,0},{8,10},{10,12},{12,14},{14,8},{16,18},{18,... | collective-permute-start | bytes 403592 | tf_op jit(solution)/shard_map/ppermute | solution.py:83
  150.5 4.1 %collective-permute-start.23 = (f32[33632]{0:T(1024)S(1)}, f32[33632]{0:T(1024)S(1)}, u32[]{:S(2)}, u32[]{:S(2)}) collective-permute-start(f32[33632]{0:T(1024)S(1)} %get-tuple-element.127), channel_id=1, source_target_pairs={{0,4},{2,6},{4,0},{6,2},{8,12},{10,14},{12,8},{14,10},{16,20},{18,... | collective-permute-start | bytes 403592 | tf_op jit(solution)/shard_map/ppermute | solution.py:83
  155.7 2.2 fusion.102
  157.9 2.3 fusion.106
  164.7 3.4 %collective-permute-start.18 = (bf16[128,2,1024]{0,2,1:T(8,128)(2,1)}, bf16[128,2,1024]{0,2,1:T(8,128)(2,1)S(1)}, u32[]{:S(2)}, u32[]{:S(2)}) collective-permute-start(bf16[128,2,1024]{0,2,1:T(8,128)(2,1)} %get-tuple-element.91), channel_id=1, source_target_pairs={{8,0},{10,2},{12,4},{14,6},{16,8},{18,10},{20,12},{22,14},{24,16},... | collective-permute-start | bytes 1572872 | tf_op jit(solution)/shard_map/ppermute | solution.py:18
  174.4 10.7 %collective-permute-done.28 = f32[8408]{0:T(1024)S(1)} collective-permute-done((f32[8408]{0:T(1024)S(1)}, f32[8408]{0:T(1024)S(1)}, u32[]{:S(2)}, u32[]{:S(2)}) %collective-permute-start.28) | collective-permute-done | bytes 33664 | tf_op jit(solution)/shard_map/ppermute | solution.py:92
  186.8 6.0 %collective-permute-start.33 = (f32[33632]{0:T(1024)S(1)}, f32[33632]{0:T(1024)S(1)}, u32[]{:S(2)}, u32[]{:S(2)}) collective-permute-start(f32[33632]{0:T(1024)S(1)} %dynamic_update_slice.35), channel_id=1, source_target_pairs={{0,6},{2,0},{4,2},{6,4},{8,14},{10,8},{12,10},{14,12},{16,22},{18,... | collective-permute-start | bytes 403592 | tf_op jit(solution)/shard_map/ppermute | solution.py:92
  193.0 2.3 dynamic-slice_bitcast_fusion
  198.1 4.1 %collective-permute-start.21 = (bf16[128,2,1024]{0,2,1:T(8,128)(2,1)}, bf16[128,2,1024]{0,2,1:T(8,128)(2,1)S(1)}, u32[]{:S(2)}, u32[]{:S(2)}) collective-permute-start(bf16[128,2,1024]{0,2,1:T(8,128)(2,1)} %get-tuple-element.92), channel_id=1, source_target_pairs={{0,8},{2,10},{4,12},{6,14},{8,16},{10,18},{12,20},{14,22},{16,24},... | collective-permute-start | bytes 1572872 | tf_op jit(solution)/shard_map/ppermute | solution.py:18
  205.8 5.7 %collective-permute-start.14 = (bf16[128,2,1024]{0,2,1:T(8,128)(2,1)}, bf16[128,2,1024]{0,2,1:T(8,128)(2,1)}, u32[]{:S(2)}, u32[]{:S(2)}) collective-permute-start(bf16[128,2,1024]{0,2,1:T(8,128)(2,1)} %get-tuple-element.101), channel_id=1, source_target_pairs={{0,4},{2,6},{4,8},{6,10},{8,12},{10,14},{12,16},{14,18},{16,20},{1... | collective-permute-start | bytes 1572872 | tf_op jit(solution)/shard_map/ppermute | solution.py:18
  218.2 7.1 %collective-permute-done.19 = bf16[128,2,1024]{0,2,1:T(8,128)(2,1)S(1)} collective-permute-done((bf16[128,2,1024]{0,2,1:T(8,128)(2,1)}, bf16[128,2,1024]{0,2,1:T(8,128)(2,1)S(1)}, u32[]{:S(2)}, u32[]{:S(2)}) %collective-permute-start.19) | collective-permute-done | bytes 524320 | tf_op jit(solution)/shard_map/ppermute | solution.py:18
  229.5 2.6 collective-permute-start.13
  234.2 2.2 fusion.96
  236.5 3.7 %collective-permute-start.16 = (bf16[128,4,1024]{0,2,1:T(8,128)(2,1)}, bf16[128,4,1024]{0,2,1:T(8,128)(2,1)S(1)}, u32[]{:S(2)}, u32[]{:S(2)}) collective-permute-start(bf16[128,4,1024]{0,2,1:T(8,128)(2,1)} %get-tuple-element.45), channel_id=1, source_target_pairs={{6,0},{8,2},{10,4},{12,6},{14,8},{16,10},{18,12},{20,14},{22,16},{... | collective-permute-start | bytes 3145736 | tf_op jit(solution)/shard_map/ppermute | solution.py:18
  240.2 23.3 %collective-permute-done.13 = bf16[128,2,1024]{0,2,1:T(8,128)(2,1)S(1)} collective-permute-done((bf16[128,2,1024]{0,2,1:T(8,128)(2,1)S(1)}, bf16[128,2,1024]{0,2,1:T(8,128)(2,1)S(1)}, u32[]{:S(2)}, u32[]{:S(2)}) %collective-permute-start.13) | collective-permute-done | bytes 524320 | tf_op jit(solution)/shard_map/ppermute | solution.py:18
  264.1 2.3 fusion.108
  269.2 2.2 fusion.104
  272.0 9.1 %collective-permute-done.10 = bf16[128,4,1024]{0,2,1:T(8,128)(2,1)S(1)} collective-permute-done((bf16[128,4,1024]{0,2,1:T(8,128)(2,1)S(1)}, bf16[128,4,1024]{0,2,1:T(8,128)(2,1)S(1)}, u32[]{:S(2)}, u32[]{:S(2)}) %collective-permute-start.10) | collective-permute-done | bytes 1048608 | tf_op jit(solution)/shard_map/ppermute | solution.py:100
  284.9 2.4 fusion.119
  291.6 16.5 %fusion.40 = f32[128,4,1024]{0,2,1:T(8,128)} fusion(f32[128,4,6]{0,2,1:T(8,128)} %get-tuple-element.72, f32[128,4,1018]{0,2,1:T(8,128)S(1)} %copy-done.21, f32[128,4,1018]{0,2,1:T(8,128)S(1)} %copy-done.20, f32[128,4,6]{0,2,1:T(8,128)} %get-tuple-element.71, f32[128,4,6]{0,2,1:T(8,128)} %get-tuple-element.68, f32[128,4,1018]{0,2,1:T(8,128)S(1)} %copy-done.19, ...), kind=kLoop, calls=%fused_computation.76 | loop fusion | flops 45088768 | bytes 50345472 | tf_op jit(solution)/shard_map/add | solution.py:196
  308.0 3.0 copy.41
  (334 shorter events, 77.6 us)
Async XLA Ops:
  0.6 30.9 %copy-start = (bf16[4,128,256]{2,1,0:T(8,128)(2,1)S(1)}, bf16[4,128,256]{2,1,0:T(8,128)(2,1)}, u32[]{:S(2)}) copy-start(bf16[4,128,256]{2,1,0:T(8,128)(2,1)} %param.6) | copy-start | bytes 786436
  3.7 45.8 %collective-permute-start.8 = (bf16[128,2,1024]{0,2,1:T(8,128)(2,1)}, bf16[128,2,1024]{0,2,1:T(8,128)(2,1)}, u32[]{:S(2)}, u32[]{:S(2)}) collective-permute-start(bf16[128,2,1024]{0,2,1:T(8,128)(2,1)} %get-tuple-element.123), channel_id=1, source_target_pairs={{8,0},{10,2},{12,4},{14,6},{16,8},{18,10},{20,12},{22,14},{24,16},... | collective-permute-start | bytes 1572872 | tf_op jit(solution)/shard_map/ppermute | solution.py:18
  6.0 28.1 %collective-permute-start.6 = (bf16[128,2,1024]{0,2,1:T(8,128)(2,1)}, bf16[128,2,1024]{0,2,1:T(8,128)(2,1)}, u32[]{:S(2)}, u32[]{:S(2)}) collective-permute-start(bf16[128,2,1024]{0,2,1:T(8,128)(2,1)} %get-tuple-element.123), channel_id=1, source_target_pairs={{0,10},{2,12},{4,14},{6,16},{8,18},{10,20},{12,22},{14,24},{16,26}... | collective-permute-start | bytes 1572872 | tf_op jit(solution)/shard_map/ppermute | solution.py:18
  9.5 49.4 %collective-permute-start.2 = (bf16[128,2,1024]{0,2,1:T(8,128)(2,1)}, bf16[128,2,1024]{0,2,1:T(8,128)(2,1)}, u32[]{:S(2)}, u32[]{:S(2)}) collective-permute-start(bf16[128,2,1024]{0,2,1:T(8,128)(2,1)} %get-tuple-element.123), channel_id=1, source_target_pairs={{2,0},{4,2},{6,4},{8,6},{10,8},{12,10},{14,12},{16,14},{18,16},{20... | collective-permute-start | bytes 1572872 | tf_op jit(solution)/shard_map/ppermute | solution.py:18
  14.3 59.5 %collective-permute-start = (bf16[128,2,1024]{0,2,1:T(8,128)(2,1)}, bf16[128,2,1024]{0,2,1:T(8,128)(2,1)}, u32[]{:S(2)}, u32[]{:S(2)}) collective-permute-start(bf16[128,2,1024]{0,2,1:T(8,128)(2,1)} %get-tuple-element.123), channel_id=1, source_target_pairs={{0,4},{2,6},{4,8},{6,10},{8,12},{10,14},{12,16},{14,18},{16,20},{1... | collective-permute-start | bytes 1572872 | tf_op jit(solution)/shard_map/ppermute | solution.py:18
  16.2 19.1 %collective-permute-start.7 = (bf16[128,2,1024]{0,2,1:T(8,128)(2,1)}, bf16[128,2,1024]{0,2,1:T(8,128)(2,1)}, u32[]{:S(2)}, u32[]{:S(2)}) collective-permute-start(bf16[128,2,1024]{0,2,1:T(8,128)(2,1)} %get-tuple-element.124), channel_id=1, source_target_pairs={{0,8},{2,10},{4,12},{6,14},{8,16},{10,18},{12,20},{14,22},{16,24},... | collective-permute-start | bytes 1572872 | tf_op jit(solution)/shard_map/ppermute | solution.py:18
  27.6 55.6 %copy-start.5 = (f32[128,4,1018]{0,2,1:T(8,128)}, f32[128,4,1018]{0,2,1:T(8,128)S(1)}, u32[]{:S(2)}) copy-start(f32[128,4,1018]{0,2,1:T(8,128)S(1)} %get-tuple-element.105) | copy-start | bytes 6254596
  34.1 21.3 %collective-permute-start.9 = (bf16[128,2,1024]{0,2,1:T(8,128)(2,1)}, bf16[128,2,1024]{0,2,1:T(8,128)(2,1)S(1)}, u32[]{:S(2)}, u32[]{:S(2)}) collective-permute-start(bf16[128,2,1024]{0,2,1:T(8,128)(2,1)} %get-tuple-element.124), channel_id=1, source_target_pairs={{10,0},{12,2},{14,4},{16,6},{18,8},{20,10},{22,12},{24,14},{26,16}... | collective-permute-start | bytes 1572872 | tf_op jit(solution)/shard_map/ppermute | solution.py:18
  35.4 36.3 %collective-permute-start.3 = (bf16[128,2,1024]{0,2,1:T(8,128)(2,1)}, bf16[128,2,1024]{0,2,1:T(8,128)(2,1)S(1)}, u32[]{:S(2)}, u32[]{:S(2)}) collective-permute-start(bf16[128,2,1024]{0,2,1:T(8,128)(2,1)} %get-tuple-element.124), channel_id=1, source_target_pairs={{4,0},{6,2},{8,4},{10,6},{12,8},{14,10},{16,12},{18,14},{20,16},{2... | collective-permute-start | bytes 1572872 | tf_op jit(solution)/shard_map/ppermute | solution.py:18
  49.4 24.4 %collective-permute-start.1 = (bf16[128,2,1024]{0,2,1:T(8,128)(2,1)}, bf16[128,2,1024]{0,2,1:T(8,128)(2,1)S(1)}, u32[]{:S(2)}, u32[]{:S(2)}) collective-permute-start(bf16[128,2,1024]{0,2,1:T(8,128)(2,1)} %get-tuple-element.124), channel_id=1, source_target_pairs={{0,2},{2,4},{4,6},{6,8},{8,10},{10,12},{12,14},{14,16},{16,18},{18... | collective-permute-start | bytes 1572872 | tf_op jit(solution)/shard_map/ppermute | solution.py:18
  55.4 20.6 %copy-start.24 = (bf16[128,2,1024]{0,2,1:T(8,128)(2,1)}, bf16[128,2,1024]{0,2,1:T(8,128)(2,1)S(1)}, u32[]{:S(2)}) copy-start(bf16[128,2,1024]{0,2,1:T(8,128)(2,1)S(1)} %collective-permute-done.9) | copy-start | bytes 1572868
  55.4 51.0 %collective-permute-start.5 = (bf16[128,4,1024]{0,2,1:T(8,128)(2,1)S(1)}, bf16[128,4,1024]{0,2,1:T(8,128)(2,1)S(1)}, u32[]{:S(2)}, u32[]{:S(2)}) collective-permute-start(bf16[128,4,1024]{0,2,1:T(8,128)(2,1)S(1)} %copy.25), channel_id=1, source_target_pairs={{6,0},{8,2},{10,4},{12,6},{14,8},{16,10},{18,12},{20,14},{22,16},{... | collective-permute-start | bytes 3145736 | tf_op jit(solution)/shard_map/ppermute | solution.py:18
  58.5 17.5 %copy-start.41 = (f32[128,4,18]{0,2,1:T(8,128)}, f32[128,4,18]{0,2,1:T(8,128)S(1)}, u32[]{:S(2)}) copy-start(f32[128,4,18]{0,2,1:T(8,128)S(1)} %get-tuple-element.88) | copy-start | bytes 110596
  58.8 17.2 %copy-start.14 = (f32[128,4,1006]{0,2,1:T(8,128)}, f32[128,4,1006]{0,2,1:T(8,128)S(1)}, u32[]{:S(2)}) copy-start(f32[128,4,1006]{0,2,1:T(8,128)S(1)} %get-tuple-element.89) | copy-start | bytes 6180868
  58.8 17.2 %copy-start.15 = (f32[128,4,1006]{0,2,1:T(8,128)}, f32[128,4,1006]{0,2,1:T(8,128)S(1)}, u32[]{:S(2)}) copy-start(f32[128,4,1006]{0,2,1:T(8,128)S(1)} %get-tuple-element.90) | copy-start | bytes 6180868
  58.9 44.3 %collective-permute-start.4 = (bf16[128,4,1024]{0,2,1:T(8,128)(2,1)S(1)}, bf16[128,4,1024]{0,2,1:T(8,128)(2,1)S(1)}, u32[]{:S(2)}, u32[]{:S(2)}) collective-permute-start(bf16[128,4,1024]{0,2,1:T(8,128)(2,1)S(1)} %copy.25), channel_id=1, source_target_pairs={{0,6},{2,8},{4,10},{6,12},{8,14},{10,16},{12,18},{14,20},{16,22},{... | collective-permute-start | bytes 3145736 | tf_op jit(solution)/shard_map/ppermute | solution.py:18
  71.7 25.2 %collective-permute-start.11 = (bf16[128,4,1024]{2,0,1:T(8,128)(2,1)}, bf16[128,4,1024]{2,0,1:T(8,128)(2,1)}, u32[]{:S(2)}, u32[]{:S(2)}) collective-permute-start(bf16[128,4,1024]{2,0,1:T(8,128)(2,1)} %copy.33), channel_id=1, source_target_pairs={{0,1},{1,0},{2,3},{3,2},{4,5},{5,4},{6,7},{7,6},{8,9},{9,8},{10,11... | collective-permute-start | bytes 3145736 | tf_op jit(solution)/shard_map/ppermute | solution.py:100
  99.4 29.1 %copy-start.2 = (bf16[4,128,4,1024]{1,3,2,0:T(8,128)(2,1)}, bf16[4,128,4,1024]{1,3,2,0:T(8,128)(2,1)S(1)}, u32[]{:S(2)}) copy-start(bf16[4,128,4,1024]{1,3,2,0:T(8,128)(2,1)S(1)} %add_convert_fusion) | copy-start | bytes 12582916
  139.0 15.7 %copy-start.28 = (bf16[128,4,1024]{0,2,1:T(8,128)(2,1)S(1)}, bf16[128,4,1024]{0,2,1:T(8,128)(2,1)}, u32[]{:S(2)}) copy-start(bf16[128,4,1024]{0,2,1:T(8,128)(2,1)} %get-tuple-element.44) | copy-start | bytes 3145732
  139.1 16.5 %copy-start.4 = (f32[128,4,1024]{0,2,1:T(8,128)S(1)}, f32[128,4,1024]{0,2,1:T(8,128)}, u32[]{:S(2)}) copy-start(f32[128,4,1024]{0,2,1:T(8,128)} %get-tuple-element.42) | copy-start | bytes 6291460
  143.9 17.0 %collective-permute-start.22 = (f32[33632]{0:T(1024)S(1)}, f32[33632]{0:T(1024)S(1)}, u32[]{:S(2)}, u32[]{:S(2)}) collective-permute-start(f32[33632]{0:T(1024)S(1)} %get-tuple-element.125), channel_id=1, source_target_pairs={{0,2},{2,4},{4,6},{6,0},{8,10},{10,12},{12,14},{14,8},{16,18},{18,... | collective-permute-start | bytes 403592 | tf_op jit(solution)/shard_map/ppermute | solution.py:83
  150.5 10.4 %collective-permute-start.24 = (f32[33632]{0:T(1024)S(1)}, f32[33632]{0:T(1024)S(1)}, u32[]{:S(2)}, u32[]{:S(2)}) collective-permute-start(f32[33632]{0:T(1024)S(1)} %get-tuple-element.126), channel_id=1, source_target_pairs={{0,6},{2,0},{4,2},{6,4},{8,14},{10,8},{12,10},{14,12},{16,22},{18,... | collective-permute-start | bytes 403592 | tf_op jit(solution)/shard_map/ppermute | solution.py:83
  150.5 10.4 %collective-permute-start.23 = (f32[33632]{0:T(1024)S(1)}, f32[33632]{0:T(1024)S(1)}, u32[]{:S(2)}, u32[]{:S(2)}) collective-permute-start(f32[33632]{0:T(1024)S(1)} %get-tuple-element.127), channel_id=1, source_target_pairs={{0,4},{2,6},{4,0},{6,2},{8,12},{10,14},{12,8},{14,10},{16,20},{18,... | collective-permute-start | bytes 403592 | tf_op jit(solution)/shard_map/ppermute | solution.py:83
  160.2 13.1 %copy-start.27 = (bf16[128,4,1024]{0,2,1:T(8,128)(2,1)S(1)}, bf16[128,4,1024]{0,2,1:T(8,128)(2,1)}, u32[]{:S(2)}) copy-start(bf16[128,4,1024]{0,2,1:T(8,128)(2,1)} %get-tuple-element.46) | copy-start | bytes 3145732
  162.0 7.5 %collective-permute-start.25 = (f32[8408]{0:T(1024)S(1)}, f32[8408]{0:T(1024)S(1)}, u32[]{:S(2)}, u32[]{:S(2)}) collective-permute-start(f32[8408]{0:T(1024)S(1)} %get-tuple-element.128), channel_id=1, source_target_pairs={{0,8},{2,10},{4,12},{6,14},{8,16},{10,18},{12,20},{14,22},{16,24},... | collective-permute-start | bytes 100904 | tf_op jit(solution)/shard_map/ppermute | solution.py:83
  162.1 7.4 %collective-permute-start.27 = (f32[8408]{0:T(1024)S(1)}, f32[8408]{0:T(1024)S(1)}, u32[]{:S(2)}, u32[]{:S(2)}) collective-permute-start(f32[8408]{0:T(1024)S(1)} %get-tuple-element.129), channel_id=1, source_target_pairs={{0,24},{2,26},{4,28},{6,30},{8,0},{10,2},{12,4},{14,6},{16,8},{18,... | collective-permute-start | bytes 100904 | tf_op jit(solution)/shard_map/ppermute | solution.py:83
  164.1 5.4 %collective-permute-start.26 = (f32[8408]{0:T(1024)S(1)}, f32[8408]{0:T(1024)S(1)}, u32[]{:S(2)}, u32[]{:S(2)}) collective-permute-start(f32[8408]{0:T(1024)S(1)} %get-tuple-element.130), channel_id=1, source_target_pairs={{0,16},{2,18},{4,20},{6,22},{8,24},{10,26},{12,28},{14,30},{16,0},... | collective-permute-start | bytes 100904 | tf_op jit(solution)/shard_map/ppermute | solution.py:83
  164.7 51.5 %collective-permute-start.18 = (bf16[128,2,1024]{0,2,1:T(8,128)(2,1)}, bf16[128,2,1024]{0,2,1:T(8,128)(2,1)S(1)}, u32[]{:S(2)}, u32[]{:S(2)}) collective-permute-start(bf16[128,2,1024]{0,2,1:T(8,128)(2,1)} %get-tuple-element.91), channel_id=1, source_target_pairs={{8,0},{10,2},{12,4},{14,6},{16,8},{18,10},{20,12},{22,14},{24,16},... | collective-permute-start | bytes 1572872 | tf_op jit(solution)/shard_map/ppermute | solution.py:18
  168.2 61.3 %collective-permute-start.20 = (bf16[128,2,1024]{0,2,1:T(8,128)(2,1)}, bf16[128,2,1024]{0,2,1:T(8,128)(2,1)S(1)}, u32[]{:S(2)}, u32[]{:S(2)}) collective-permute-start(bf16[128,2,1024]{0,2,1:T(8,128)(2,1)} %get-tuple-element.91), channel_id=1, source_target_pairs={{0,10},{2,12},{4,14},{6,16},{8,18},{10,20},{12,22},{14,24},{16,26}... | collective-permute-start | bytes 1572872 | tf_op jit(solution)/shard_map/ppermute | solution.py:18
  169.9 15.8 %collective-permute-start.29 = (f32[8408]{0:T(1024)S(1)}, f32[8408]{0:T(1024)S(1)}, u32[]{:S(2)}, u32[]{:S(2)}) collective-permute-start(f32[8408]{0:T(1024)S(1)} %get-tuple-element.40), channel_id=1, source_target_pairs={{0,16},{2,18},{4,20},{6,22},{8,24},{10,26},{12,28},{14,30},{16,0},... | collective-permute-start | bytes 100904 | tf_op jit(solution)/shard_map/ppermute | solution.py:92
  171.3 13.8 %collective-permute-start.28 = (f32[8408]{0:T(1024)S(1)}, f32[8408]{0:T(1024)S(1)}, u32[]{:S(2)}, u32[]{:S(2)}) collective-permute-start(f32[8408]{0:T(1024)S(1)} %get-tuple-element.40), channel_id=1, source_target_pairs={{0,8},{2,10},{4,12},{6,14},{8,16},{10,18},{12,20},{14,22},{16,24},... | collective-permute-start | bytes 100904 | tf_op jit(solution)/shard_map/ppermute | solution.py:92
  171.3 14.8 %collective-permute-start.30 = (f32[8408]{0:T(1024)S(1)}, f32[8408]{0:T(1024)S(1)}, u32[]{:S(2)}, u32[]{:S(2)}) collective-permute-start(f32[8408]{0:T(1024)S(1)} %get-tuple-element.40), channel_id=1, source_target_pairs={{0,24},{2,26},{4,28},{6,30},{8,0},{10,2},{12,4},{14,6},{16,8},{18,... | collective-permute-start | bytes 100904 | tf_op jit(solution)/shard_map/ppermute | solution.py:92
  186.8 19.1 %collective-permute-start.33 = (f32[33632]{0:T(1024)S(1)}, f32[33632]{0:T(1024)S(1)}, u32[]{:S(2)}, u32[]{:S(2)}) collective-permute-start(f32[33632]{0:T(1024)S(1)} %dynamic_update_slice.35), channel_id=1, source_target_pairs={{0,6},{2,0},{4,2},{6,4},{8,14},{10,8},{12,10},{14,12},{16,22},{18,... | collective-permute-start | bytes 403592 | tf_op jit(solution)/shard_map/ppermute | solution.py:92
  192.8 10.5 %collective-permute-start.32 = (f32[33632]{0:T(1024)S(1)}, f32[33632]{0:T(1024)S(1)}, u32[]{:S(2)}, u32[]{:S(2)}) collective-permute-start(f32[33632]{0:T(1024)S(1)} %dynamic_update_slice.35), channel_id=1, source_target_pairs={{0,4},{2,6},{4,0},{6,2},{8,12},{10,14},{12,8},{14,10},{16,20},{18,... | collective-permute-start | bytes 403592 | tf_op jit(solution)/shard_map/ppermute | solution.py:92
  192.8 5.3 %collective-permute-start.31 = (f32[33632]{0:T(1024)S(1)}, f32[33632]{0:T(1024)S(1)}, u32[]{:S(2)}, u32[]{:S(2)}) collective-permute-start(f32[33632]{0:T(1024)S(1)} %dynamic_update_slice.35), channel_id=1, source_target_pairs={{0,2},{2,4},{4,6},{6,0},{8,10},{10,12},{12,14},{14,8},{16,18},{18,... | collective-permute-start | bytes 403592 | tf_op jit(solution)/shard_map/ppermute | solution.py:92
  198.1 34.0 %collective-permute-start.21 = (bf16[128,2,1024]{0,2,1:T(8,128)(2,1)}, bf16[128,2,1024]{0,2,1:T(8,128)(2,1)S(1)}, u32[]{:S(2)}, u32[]{:S(2)}) collective-permute-start(bf16[128,2,1024]{0,2,1:T(8,128)(2,1)} %get-tuple-element.92), channel_id=1, source_target_pairs={{0,8},{2,10},{4,12},{6,14},{8,16},{10,18},{12,20},{14,22},{16,24},... | collective-permute-start | bytes 1572872 | tf_op jit(solution)/shard_map/ppermute | solution.py:18
  203.3 21.9 %collective-permute-start.19 = (bf16[128,2,1024]{0,2,1:T(8,128)(2,1)}, bf16[128,2,1024]{0,2,1:T(8,128)(2,1)S(1)}, u32[]{:S(2)}, u32[]{:S(2)}) collective-permute-start(bf16[128,2,1024]{0,2,1:T(8,128)(2,1)} %get-tuple-element.92), channel_id=1, source_target_pairs={{10,0},{12,2},{14,4},{16,6},{18,8},{20,10},{22,12},{24,14},{26,16}... | collective-permute-start | bytes 1572872 | tf_op jit(solution)/shard_map/ppermute | solution.py:18
  205.8 61.9 %collective-permute-start.14 = (bf16[128,2,1024]{0,2,1:T(8,128)(2,1)}, bf16[128,2,1024]{0,2,1:T(8,128)(2,1)}, u32[]{:S(2)}, u32[]{:S(2)}) collective-permute-start(bf16[128,2,1024]{0,2,1:T(8,128)(2,1)} %get-tuple-element.101), channel_id=1, source_target_pairs={{0,4},{2,6},{4,8},{6,10},{8,12},{10,14},{12,16},{14,18},{16,20},{1... | collective-permute-start | bytes 1572872 | tf_op jit(solution)/shard_map/ppermute | solution.py:18
  216.3 13.2 %copy-start.29 = (bf16[128,2,1024]{0,2,1:T(8,128)(2,1)}, bf16[128,2,1024]{0,2,1:T(8,128)(2,1)S(1)}, u32[]{:S(2)}) copy-start(bf16[128,2,1024]{0,2,1:T(8,128)(2,1)S(1)} %collective-permute-done.18) | copy-start | bytes 1572868
  216.3 20.2 %collective-permute-start.12 = (bf16[128,2,1024]{0,2,1:T(8,128)(2,1)}, bf16[128,2,1024]{0,2,1:T(8,128)(2,1)S(1)}, u32[]{:S(2)}, u32[]{:S(2)}) collective-permute-start(bf16[128,2,1024]{0,2,1:T(8,128)(2,1)} %get-tuple-element.101), channel_id=1, source_target_pairs={{2,0},{4,2},{6,4},{8,6},{10,8},{12,10},{14,12},{16,14},{18,16},{20... | collective-permute-start | bytes 1572872 | tf_op jit(solution)/shard_map/ppermute | solution.py:18
  225.2 42.5 %collective-permute-start.15 = (bf16[128,2,1024]{0,2,1:T(8,128)(2,1)}, bf16[128,2,1024]{0,2,1:T(8,128)(2,1)S(1)}, u32[]{:S(2)}, u32[]{:S(2)}) collective-permute-start(bf16[128,2,1024]{0,2,1:T(8,128)(2,1)} %get-tuple-element.102), channel_id=1, source_target_pairs={{0,2},{2,4},{4,6},{6,8},{8,10},{10,12},{12,14},{14,16},{16,18},{18... | collective-permute-start | bytes 1572872 | tf_op jit(solution)/shard_map/ppermute | solution.py:18
  229.5 34.0 %collective-permute-start.13 = (bf16[128,2,1024]{0,2,1:T(8,128)(2,1)S(1)}, bf16[128,2,1024]{0,2,1:T(8,128)(2,1)S(1)}, u32[]{:S(2)}, u32[]{:S(2)}) collective-permute-start(bf16[128,2,1024]{0,2,1:T(8,128)(2,1)S(1)} %copy-done.40), channel_id=1, source_target_pairs={{4,0},{6,2},{8,4},{10,6},{12,8},{14,10},{16,12},{18,14},{20,16},{2... | collective-permute-start | bytes 1572872 | tf_op jit(solution)/shard_map/ppermute | solution.py:18
  232.1 52.6 %collective-permute-start.17 = (bf16[128,4,1024]{0,2,1:T(8,128)(2,1)}, bf16[128,4,1024]{0,2,1:T(8,128)(2,1)S(1)}, u32[]{:S(2)}, u32[]{:S(2)}) collective-permute-start(bf16[128,4,1024]{0,2,1:T(8,128)(2,1)} %get-tuple-element.45), channel_id=1, source_target_pairs={{0,6},{2,8},{4,10},{6,12},{8,14},{10,16},{12,18},{14,20},{16,22},{... | collective-permute-start | bytes 3145736 | tf_op jit(solution)/shard_map/ppermute | solution.py:18
  234.2 29.3 %copy-start.39 = (bf16[128,4,1024]{0,2,1:T(8,128)(2,1)S(1)}, bf16[128,4,1024]{0,2,1:T(8,128)(2,1)}, u32[]{:S(2)}) copy-start(bf16[128,4,1024]{0,2,1:T(8,128)(2,1)} %dynamic-slice_bitcast_fusion) | copy-start | bytes 3145732
  236.5 30.0 %copy-start.33 = (bf16[128,2,1024]{0,2,1:T(8,128)(2,1)}, bf16[128,2,1024]{0,2,1:T(8,128)(2,1)S(1)}, u32[]{:S(2)}) copy-start(bf16[128,2,1024]{0,2,1:T(8,128)(2,1)S(1)} %collective-permute-done.12) | copy-start | bytes 1572868
  236.5 46.6 %collective-permute-start.16 = (bf16[128,4,1024]{0,2,1:T(8,128)(2,1)}, bf16[128,4,1024]{0,2,1:T(8,128)(2,1)S(1)}, u32[]{:S(2)}, u32[]{:S(2)}) collective-permute-start(bf16[128,4,1024]{0,2,1:T(8,128)(2,1)} %get-tuple-element.45), channel_id=1, source_target_pairs={{6,0},{8,2},{10,4},{12,6},{14,8},{16,10},{18,12},{20,14},{22,16},{... | collective-permute-start | bytes 3145736 | tf_op jit(solution)/shard_map/ppermute | solution.py:18
  263.5 17.7 %collective-permute-start.10 = (bf16[128,4,1024]{0,2,1:T(8,128)(2,1)S(1)}, bf16[128,4,1024]{0,2,1:T(8,128)(2,1)S(1)}, u32[]{:S(2)}, u32[]{:S(2)}) collective-permute-start(bf16[128,4,1024]{0,2,1:T(8,128)(2,1)S(1)} %copy-done.39), channel_id=1, source_target_pairs={{0,1},{1,0},{2,3},{3,2},{4,5},{5,4},{6,7},{7,6},{8,9},{9,8},{10,11... | collective-permute-start | bytes 3145736 | tf_op jit(solution)/shard_map/ppermute | solution.py:100
  291.6 19.5 %copy-start.1 = (bf16[4,128,256]{2,1,0:T(8,128)(2,1)S(1)}, bf16[4,128,256]{2,1,0:T(8,128)(2,1)}, u32[]{:S(2)}) copy-start(bf16[4,128,256]{2,1,0:T(8,128)(2,1)} %param.6) | copy-start | bytes 786436
  (94 other events, 398.2 us)
